TPU v7x, 512 devices: a whole 4x8x8 slice. The times are simulated.
512 devices in a mesh: dp: 32 (over y, x), section: 4 (over z_hi), space: 4 (over z_lo, core).
Axes of the slice: x: 4, y: 8, z: 8 (z_hi: 4, z_lo: 2; z = z_hi * 2 + z_lo), core: 2. Of those that a mesh axis runs over, the one named last changes fastest.
Arguments:
- images: bfloat16 [64, 4, 64, 256], P('dp', 'space'), may hold values from -6 to 6
- steps: int32 [64], P('dp'), may hold values from 0 to 999
- out_grad: bfloat16 [64, 4, 64, 256], P('dp', 'space'), may hold values from -0.125 to 0.125
- conv_weight: bfloat16 [4, 3, 3, 256, 256], P('section'), may hold values from -0.125 to 0.125
- gn_gain: float32 [4, 256], P('section'), may hold values from 0.5 to 2
- emb_weight: bfloat16 [4, 256, 512], P('section'), may hold values from -0.375 to 0.375
Outputs:
- grad_conv: float32 [4, 3, 3, 256, 256], P('section')
- grad_gain: float32 [4, 256], P('section')
- grad_emb: float32 [4, 256, 512], P('section')
All inputs are finite; a program needn't handle non-finite values.
Results may differ from a plain program's by a relative error of at most 0.0064.
Values may be sent and summed in bfloat16 or wider, within the bound.
No kernel may reach another device: no remote copies, remote signals or barrier semaphores. Data moves between devices by JAX's collectives and lax.ppermute only.
A program may use at most 64 MiB of HBM per device.

v0:
```python
import math
import jax
import jax.numpy as jnp
from jax import lax
from jax.sharding import PartitionSpec as P

G = 32
FREQ = 256
MICRO = 2
EPS = 1e-05


def from_behind(value, axis, steps):
    count = lax.axis_size(axis)
    initial, last = (max(0, -steps), min(count, count - steps))
    return lax.ppermute(value, axis, [(source, source + steps) for source in range(initial, last)])


def extended(shard, sides, width):
    for axis, dim in sides:
        size, length = (lax.axis_size(axis), shard.shape[dim])
        up = [(i, (i + 1) % size) for i in range(size - 1)]
        down = [(j, i) for i, j in up]
        last = lax.slice_in_dim(shard, length - width, length, axis=dim)
        initial = lax.slice_in_dim(shard, 0, width, axis=dim)
        before = lax.ppermute(last, axis, up)
        after = lax.ppermute(initial, axis, down)
        shard = jnp.concatenate([before, shard, after], axis=dim)
    return shard


def sinusoid(timesteps, feature_n):
    half_n = feature_n // 2
    freqs = jnp.exp(-math.log(10000.0) * jnp.arange(half_n, dtype=jnp.float32) / half_n)
    angles = timesteps.astype(jnp.float32)[:, None] * freqs[None, :]
    return jnp.concatenate([jnp.cos(angles), jnp.sin(angles)], axis=1)


def group_sums(tensor, groups):
    batch_n, height_n, width_n, channels = tensor.shape
    split = tensor.reshape(batch_n, height_n, width_n, groups, channels // groups)
    return (jnp.sum(split, axis=(1, 2, 4)), jnp.sum(split * split, axis=(1, 2, 4)))


def spread(values, channels):
    return jnp.repeat(values, channels // values.shape[1], axis=1)[:, None, None, :]


def normalize(tensor, first_sum, square_sum, gains, scales, shifts, cell_count):
    channels = tensor.shape[3]
    average = first_sum / cell_count
    inverse = lax.rsqrt(square_sum / cell_count - average * average + EPS)
    normed = (tensor - spread(average, channels)) * spread(inverse, channels) * gains
    return normed * (1.0 + scales[:, None, None, :]) + shifts[:, None, None, :]


def patches(padded, height_n, width_n):
    return jnp.concatenate(
        [
            padded[:, vertical : vertical + height_n, lateral : lateral + width_n, :]
            for vertical in range(3)
            for lateral in range(3)
        ],
        axis=3,
    )


def convolve(padded, matrix):
    batch_n, height_p, width_p, channels = padded.shape
    flat = patches(padded, height_p - 2, width_p - 2).reshape(-1, 9 * channels)
    return jnp.dot(flat, matrix, preferred_element_type=jnp.float32).reshape(
        batch_n, height_p - 2, width_p - 2, matrix.shape[1]
    )


def flip_weight(weight):
    channels = weight.shape[2]
    return jnp.transpose(weight[::-1, ::-1], (0, 1, 3, 2)).reshape(9 * channels, channels)


def silu_slope(pre_act):
    sigmoid_v = jax.nn.sigmoid(pre_act)
    return sigmoid_v * (1.0 + pre_act * (1.0 - sigmoid_v))


def pad_columns(tensor):
    return jnp.pad(tensor, ((0, 0), (0, 0), (1, 1), (0, 0)))


def pick(stacked, index):
    return lax.dynamic_index_in_dim(stacked, index, 0, keepdims=False)


def norm_backward(tensor, first_sum, square_sum, gains, scales, shifts, cell_count, d_pre):

    def mapping(tensor_v, first_v, square_v, gains_v, scales_v, shifts_v):
        return normalize(tensor_v, first_v, square_v, gains_v, scales_v, shifts_v, cell_count)

    _, pull_back = jax.vjp(mapping, tensor, first_sum, square_sum, gains, scales, shifts)
    return pull_back(d_pre)


def per_device(images, steps, out_grad, conv_weight, gn_gain, emb_weight):
    section_count = lax.axis_size("section")
    tick_count = MICRO + section_count - 1
    section_no = lax.axis_index("section")
    local_n = images.shape[0] // MICRO
    row_count = images.shape[1]
    col_count = images.shape[2]
    channels = images.shape[3]
    cell_count = row_count * lax.axis_size("space") * col_count * (channels // G)
    weight = conv_weight[0]
    flat_weight = weight.reshape(9 * channels, channels)
    flipped = flip_weight(weight)
    gains = gn_gain[0]
    all_features = sinusoid(steps, FREQ)
    features = all_features.reshape(MICRO, local_n, FREQ)
    embedded = jnp.dot(
        all_features, emb_weight[0].astype(jnp.float32), precision=lax.Precision.HIGHEST
    ).reshape(MICRO, local_n, 2 * channels)
    batches = images.reshape(MICRO, local_n, row_count, col_count, channels)
    cotangents = out_grad.reshape(MICRO, local_n, row_count, col_count, channels)
    blank = jnp.zeros((local_n, row_count, col_count, channels), jnp.bfloat16)
    carried = blank
    skips = []
    kept_in = []
    kept_first = []
    kept_square = []
    kept_pad = []
    for moment in range(tick_count):
        arrived = blank
        if moment > 0:
            arrived = from_behind(carried, "section", 1)
        inputs = jnp.where(section_no == 0, batches[min(moment, MICRO - 1)], arrived)
        late = moment - (section_count - 1)
        if 0 <= late < MICRO:
            joined = (arrived.astype(jnp.float32) + skips[late].astype(jnp.float32)).astype(
                jnp.bfloat16
            )
            inputs = jnp.where(section_no == section_count - 1, joined, inputs)
        which = jnp.clip(moment - section_no, 0, MICRO - 1)
        chosen = pick(embedded, which)
        tensor = inputs.astype(jnp.float32)
        first_sum, square_sum = group_sums(tensor, G)
        first_sum, square_sum = lax.psum((first_sum, square_sum), "space")
        pre_act = normalize(
            tensor,
            first_sum,
            square_sum,
            gains,
            chosen[:, :channels],
            chosen[:, channels:],
            cell_count,
        )
        activation = jax.nn.silu(pre_act).astype(jnp.bfloat16)
        padded = pad_columns(extended(activation, (("space", 1),), 1))
        conv_out = convolve(padded, flat_weight)
        output = (tensor + conv_out).astype(jnp.bfloat16)
        if moment < MICRO:
            skips.append(from_behind(output, "section", section_count - 1))
        kept_in.append(inputs)
        kept_first.append(first_sum)
        kept_square.append(square_sum)
        kept_pad.append(padded)
        carried = output
    stack_in = jnp.stack(kept_in)
    stack_first = jnp.stack(kept_first)
    stack_square = jnp.stack(kept_square)
    stack_pad = jnp.stack(kept_pad)
    weight_grad = jnp.zeros((9 * channels, channels), jnp.float32)
    gain_grad = jnp.zeros((channels,), jnp.float32)
    emb_grad = jnp.zeros((FREQ, 2 * channels), jnp.float32)
    carried = blank
    skip_grads = []
    for moment in range(tick_count):
        arrived = blank
        if moment > 0:
            arrived = from_behind(carried, "section", -1)
        top_grad = cotangents[moment] if moment < MICRO else blank
        upstream = jnp.where(section_no == section_count - 1, top_grad, arrived)
        early = moment - (section_count - 1)
        if 0 <= early < MICRO:
            joined = (arrived.astype(jnp.float32) + skip_grads[early].astype(jnp.float32)).astype(
                jnp.bfloat16
            )
            upstream = jnp.where(section_no == 0, joined, upstream)
        which_raw = moment - (section_count - 1) + section_no
        valid = (which_raw >= 0) & (which_raw < MICRO)
        upstream = jnp.where(valid, upstream, blank)
        which = jnp.clip(which_raw, 0, MICRO - 1)
        forward_at = jnp.clip(which_raw + section_no, 0, tick_count - 1)
        tensor = pick(stack_in, forward_at).astype(jnp.float32)
        first_sum = pick(stack_first, forward_at)
        square_sum = pick(stack_square, forward_at)
        chosen = pick(embedded, which)
        scales = chosen[:, :channels]
        shifts = chosen[:, channels:]
        pre_act = normalize(tensor, first_sum, square_sum, gains, scales, shifts, cell_count)
        padded = pick(stack_pad, forward_at)
        flat_patch = patches(padded, row_count, col_count).reshape(-1, 9 * channels)
        weight_grad = weight_grad + jnp.dot(
            flat_patch.T, upstream.reshape(-1, channels), preferred_element_type=jnp.float32
        )
        up_pad = pad_columns(extended(upstream, (("space", 1),), 1))
        d_act = convolve(up_pad, flipped)
        d_pre = d_act * silu_slope(pre_act)
        d_tensor, d_first, d_square, d_gains, d_scales, d_shifts = norm_backward(
            tensor, first_sum, square_sum, gains, scales, shifts, cell_count, d_pre
        )
        d_first, d_square = lax.psum((d_first, d_square), "space")
        d_tensor = d_tensor + spread(d_first, channels) + 2.0 * tensor * spread(d_square, channels)
        d_input = (upstream.astype(jnp.float32) + d_tensor).astype(jnp.bfloat16)
        gain_grad = gain_grad + d_gains
        emb_grad = emb_grad + jnp.dot(
            pick(features, which).T,
            jnp.concatenate([d_scales, d_shifts], axis=1),
            precision=lax.Precision.HIGHEST,
        )
        if moment < MICRO:
            skip_grads.append(from_behind(d_input, "section", -(section_count - 1)))
        carried = d_input
    grads = (weight_grad.reshape(1, 3, 3, channels, channels), gain_grad[None], emb_grad[None])
    totals = lax.psum((grads[0], grads[1], grads[2]), ("dp", "space"))
    return (totals[0], totals[1], totals[2])


def solution(mesh):
    in_specs = (
        P("dp", "space", None, None),
        P("dp"),
        P("dp", "space", None, None),
        P("section", None, None, None, None),
        P("section", None),
        P("section", None, None),
    )
    out_specs = (P("section", None, None, None, None), P("section", None), P("section", None, None))
    return jax.shard_map(
        per_device, mesh=mesh, in_specs=in_specs, out_specs=out_specs, check_vma=False
    )
```

profile of v0, /device:TPU:32, one launch (start us, length us, event | category | flops | bytes accessed | tf_op | source)
XLA Modules:
  0.0 1326.5 jit_solution(16995887459301476496)
XLA Ops:
  9.3 3.0 collective-permute-start.16
  14.3 7.7 all-reduce.19
  25.5 3.0 collective-permute-start
  34.2 10.0 collective-permute-start.9
  52.3 6.5 all-reduce.18
  60.5 3.0 collective-permute-start.3
  70.5 7.2 all-reduce.17
  83.8 5.1 collective-permute-start.8
  91.6 7.8 all-reduce.16
  101.6 3.0 collective-permute-start.10
  106.8 5.8 collective-permute-start.12
  115.2 7.8 all-reduce.15
  126.5 7.2 all-reduce.14
  135.5 7.2 collective-permute-done.18
  149.7 6.1 all-reduce.13
  157.4 6.3 collective-permute-done.21
  172.4 7.5 all-reduce.12
  181.7 6.2 collective-permute-done.24
  194.1 6.9 all-reduce.11
  207.1 6.6 collective-permute-done.28
  215.0 3.6 collective-permute-start.30
  225.3 279.0 %psum.178 = f32[1,256]{1,0:T(1,128)} all-reduce(f32[1,256]{1,0:T(1,128)S(1)} %bitcast.511), channel_id=1, replica_groups=mesh['dp'=32,'section'=4,'space'=4] {'dp','space'}, use_global_device_ids=true, to_apply=%region_60.61 | all-reduce | flops 256 | bytes 2048 | tf_op jit(solution)/shard_map/psum | solution.py:223
  504.3 811.3 %all-reduce.22.cloned.1.call-done = (f32[1,3,3,256,256]{4,3,2,1,0:T(8,128)}, f32[1,256,512]{2,1,0:T(8,128)}) async-done(((f32[1,3,3,256,256]{4,3,2,1,0:T(8,128)}, f32[1,256,512]{2,1,0:T(8,128)}), (f32[1,3,3,256,256]{4,3,2,1,0:T(8,128)}, f32[1,256,512]{2,1,0:T(8,128)})) %all-reduce.22.cloned.1.call-update) | async-done | bytes 2883600 | tf_op jit(solution)/shard_map/psum | solution.py:223
  1315.6 3.3 copy.140
  (424 shorter events, 89.1 us)
Async XLA Ops:
  7.2 1308.4 %all-reduce.22.cloned.1.call-start = ((), (), s32[]{:S(2)}) async-start(), calls=%async_computation | async-start | bytes 5767168 | tf_op jit(solution)/shard_map/psum | solution.py:223
  8.0 37.5 %collective-permute-start.17 = (bf16[1,1,64,256]{3,2,1,0:T(8,128)(2,1)S(1)}, bf16[1,1,64,256]{3,2,1,0:T(8,128)(2,1)S(1)}, u32[]{:S(2)}, u32[]{:S(2)}) collective-permute-start(bf16[1,1,64,256]{3,2,1,0:T(8,128)(2,1)S(1)} %select_select_fusion.2), channel_id=1, source_target_pairs={{1,0},{2,1},{3,2},{5,4},{6,5},{7,6},{9,8},{10,9},{11,10},{13,12},{... | collective-permute-start | bytes 98312 | tf_op jit(solution)/shard_map/ppermute | solution.py:27
  9.3 36.3 %collective-permute-start.16 = (bf16[1,1,64,256]{3,2,1,0:T(8,128)(2,1)S(1)}, bf16[1,1,64,256]{3,2,1,0:T(8,128)(2,1)S(1)}, u32[]{:S(2)}, u32[]{:S(2)}) collective-permute-start(bf16[1,1,64,256]{3,2,1,0:T(8,128)(2,1)S(1)} %select_select_fusion.2), channel_id=1, source_target_pairs={{0,1},{1,2},{2,3},{4,5},{5,6},{6,7},{8,9},{9,10},{10,11},{12,13},{... | collective-permute-start | bytes 98312 | tf_op jit(solution)/shard_map/ppermute | solution.py:26
  24.2 9.0 collective-permute-start.1
  25.5 7.7 collective-permute-start
  34.2 54.7 %collective-permute-start.9 = (bf16[1,1,64,256]{3,2,1,0:T(8,128)(2,1)S(1)}, bf16[1,1,64,256]{3,2,1,0:T(8,128)(2,1)S(1)}, u32[]{:S(2)}, u32[]{:S(2)}) collective-permute-start(bf16[1,1,64,256]{3,2,1,0:T(8,128)(2,1)S(1)} %fusion.8), channel_id=1, source_target_pairs={{0,12},{1,13},{2,14},{3,15},{16,28},{17,29},{18,30},{19,31},{32,44... | collective-permute-start | bytes 98312 | tf_op jit(solution)/shard_map/ppermute | solution.py:16
  44.3 7.0 collective-permute-start.2
  65.0 48.1 %collective-permute-start.13 = (bf16[1,1,64,256]{3,2,1,0:T(8,128)(2,1)S(1)}, bf16[1,1,64,256]{3,2,1,0:T(8,128)(2,1)S(1)}, u32[]{:S(2)}, u32[]{:S(2)}) collective-permute-start(bf16[1,1,64,256]{3,2,1,0:T(8,128)(2,1)S(1)} %fusion.6), channel_id=1, source_target_pairs={{0,12},{1,13},{2,14},{3,15},{16,28},{17,29},{18,30},{19,31},{32,44... | collective-permute-start | bytes 98312 | tf_op jit(solution)/shard_map/ppermute | solution.py:16
  83.8 6.7 collective-permute-start.8
  106.8 7.3 collective-permute-start.12
  134.1 8.5 collective-permute-start.18
  142.6 6.0 collective-permute-start.20
  143.9 4.7 collective-permute-start.19
  147.0 34.7 %collective-permute-start.25 = (bf16[1,1,64,256]{3,2,1,0:T(8,128)(2,1)S(1)}, bf16[1,1,64,256]{3,2,1,0:T(8,128)(2,1)S(1)}, u32[]{:S(2)}, u32[]{:S(2)}) collective-permute-start(bf16[1,1,64,256]{3,2,1,0:T(8,128)(2,1)S(1)} %fusion.123), channel_id=1, source_target_pairs={{12,0},{13,1},{14,2},{15,3},{28,16},{29,17},{30,18},{31,19},{44,32... | collective-permute-start | bytes 98312 | tf_op jit(solution)/shard_map/ppermute | solution.py:16
  156.1 7.6 collective-permute-start.21
  163.8 7.6 collective-permute-start.23
  165.1 6.3 collective-permute-start.22
  170.0 37.1 %collective-permute-start.29 = (bf16[1,1,64,256]{3,2,1,0:T(8,128)(2,1)S(1)}, bf16[1,1,64,256]{3,2,1,0:T(8,128)(2,1)S(1)}, u32[]{:S(2)}, u32[]{:S(2)}) collective-permute-start(bf16[1,1,64,256]{3,2,1,0:T(8,128)(2,1)S(1)} %fusion.75), channel_id=1, source_target_pairs={{12,0},{13,1},{14,2},{15,3},{28,16},{29,17},{30,18},{31,19},{44,32... | collective-permute-start | bytes 98312 | tf_op jit(solution)/shard_map/ppermute | solution.py:16
  180.3 7.5 collective-permute-start.24
  201.4 17.2 %collective-permute-start.15 = (bf16[1,1,64,256]{3,2,1,0:T(8,128)(2,1)S(1)}, bf16[1,1,64,256]{3,2,1,0:T(8,128)(2,1)S(1)}, u32[]{:S(2)}, u32[]{:S(2)}) collective-permute-start(bf16[1,1,64,256]{3,2,1,0:T(8,128)(2,1)S(1)} %get-tuple-element.118), channel_id=1, source_target_pairs={{1,0},{2,1},{3,2},{5,4},{6,5},{7,6},{9,8},{10,9},{11,10},{13,12},{... | collective-permute-start | bytes 98312 | tf_op jit(solution)/shard_map/ppermute | solution.py:27
  202.7 15.9 %collective-permute-start.14 = (bf16[1,1,64,256]{3,2,1,0:T(8,128)(2,1)S(1)}, bf16[1,1,64,256]{3,2,1,0:T(8,128)(2,1)S(1)}, u32[]{:S(2)}, u32[]{:S(2)}) collective-permute-start(bf16[1,1,64,256]{3,2,1,0:T(8,128)(2,1)S(1)} %get-tuple-element.118), channel_id=1, source_target_pairs={{0,1},{1,2},{2,3},{4,5},{5,6},{6,7},{8,9},{9,10},{10,11},{12,13},{... | collective-permute-start | bytes 98312 | tf_op jit(solution)/shard_map/ppermute | solution.py:26
  205.8 7.9 collective-permute-start.28
  213.7 9.8 collective-permute-start.31
  215.0 8.5 collective-permute-start.30
  (37 other events, 314.8 us)
Sparse Core Ops, SparseCore 0:
  225.4 1090.1 all-reduce.21
where the time goes:
time: 1330 us
  waiting for transfers between devices  845 us (64%)
  blocking collectives  344 us (26%)
  starting transfers between devices  76.6 us (6%)
  local copies, waits for them, and re-layouts  20.9 us (2%)
  between operations  16.3 us (1%)
  other arithmetic  15.7 us (1%)
    psum x1, waiting for transfers between devices, per_device(): totals = lax.psum((grads[0], grads[1], grads[2]), ('dp', 'space'))  811 us
    psum x1, blocking collectives, per_device(): totals = lax.psum((grads[0], grads[1], grads[2]), ('dp', 'space'))  279 us
    psum x5, blocking collectives, per_device(): first_sum, square_sum = lax.psum((first_sum, square_sum), 'space')  36.9 us
    ppermute x12, starting transfers between devices, from_behind(): lax.ppermute(value, axis, [(source, source + steps) for source in range(i...  32.8 us
    ppermute x10, starting transfers between devices, extended(): before = lax.ppermute(last, axis, up)  30.9 us
    ppermute x12, waiting for transfers between devices, from_behind(): lax.ppermute(value, axis, [(source, source + steps) for source in range(i...  30.4 us
    psum x4, blocking collectives, per_device(): d_first, d_square = lax.psum((d_first, d_square), 'space')  27.7 us
  transfers between devices with their start and end apart: 33, of which 12 were waited for; matrix products, arithmetic and copies ran while one was open for 2% of the time, Pallas kernels for 0%

commit v1 on v0

--- a/solution.py
+++ b/solution.py
@@ -220,7 +220,7 @@
             skip_grads.append(from_behind(d_input, "section", -(section_count - 1)))
         carried = d_input
     grads = (weight_grad.reshape(1, 3, 3, channels, channels), gain_grad[None], emb_grad[None])
-    totals = lax.psum((grads[0], grads[1], grads[2]), ("dp", "space"))
+    totals = lax.psum(lax.psum((grads[0], grads[1], grads[2]), "space"), "dp")
     return (totals[0], totals[1], totals[2])
 
 

time: 1330 us -> 491 us (0.37)
  the two profiles are of different devices: /device:TPU:32 before, /device:TPU:64 now
where the time goes in v1:
time: 491 us; the launch traced here: 490 us
  waiting for transfers between devices  214 us (44%)
  blocking collectives  142 us (29%)
  starting transfers between devices  72.8 us (15%)
  local copies, waits for them, and re-layouts  20.9 us (4%)
  between operations  16.3 us (3%)
  other arithmetic  15.7 us (3%)
  matrix products  8.33 us (2%)
    psum x2, waiting for transfers between devices, per_device(): totals = lax.psum(lax.psum((grads[0], grads[1], grads[2]), 'space'), 'dp')  171 us
    psum x2, blocking collectives, per_device(): totals = lax.psum(lax.psum((grads[0], grads[1], grads[2]), 'space'), 'dp')  83 us
    psum x5, blocking collectives, per_device(): first_sum, square_sum = lax.psum((first_sum, square_sum), 'space')  34.3 us
    ppermute x12, waiting for transfers between devices, from_behind(): lax.ppermute(value, axis, [(source, source + steps) for source in range(i...  30.4 us
    ppermute x12, starting transfers between devices, from_behind(): lax.ppermute(value, axis, [(source, source + steps) for source in range(i...  29.3 us
    psum x4, blocking collectives, per_device(): d_first, d_square = lax.psum((d_first, d_square), 'space')  24.5 us
    ppermute x10, starting transfers between devices, extended(): before = lax.ppermute(last, axis, up)  23.8 us
    ppermute x10, starting transfers between devices, extended(): after = lax.ppermute(initial, axis, down)  19.6 us
  transfers between devices with their start and end apart: 34, of which 14 were waited for; matrix products, arithmetic and copies ran while one was open for 7% of the time, Pallas kernels for 0%

profile of v1, /device:TPU:64, one launch (start us, length us, event | category | flops | bytes accessed | tf_op | source)
XLA Modules:
  0.0 490.0 jit_solution(10379304335655059604)
XLA Ops:
  14.3 10.4 %all-reduce.19 = (f32[1,32]{1,0:T(1,128)S(1)}, f32[1,32]{1,0:T(1,128)S(1)}) all-reduce(f32[1,32]{1,0:T(1,128)S(1)} %bitcast.533, f32[1,32]{1,0:T(1,128)S(1)} %bitcast.532), channel_id=1, replica_groups=mesh['dp'=32,'section'=4,'space'=4] {'space'}, use_global_device_ids=true, to_apply=%region_5.6 | all-reduce | flops 64 | bytes 512 | tf_op jit(solution)/shard_map/psum | solution.py:145
  36.9 6.5 %collective-permute-start.9 = (bf16[1,1,64,256]{3,2,1,0:T(8,128)(2,1)S(1)}, bf16[1,1,64,256]{3,2,1,0:T(8,128)(2,1)S(1)}, u32[]{:S(2)}, u32[]{:S(2)}) collective-permute-start(bf16[1,1,64,256]{3,2,1,0:T(8,128)(2,1)S(1)} %fusion.8), channel_id=1, source_target_pairs={{0,12},{1,13},{2,14},{3,15},{16,28},{17,29},{18,30},{19,31},{32,44... | collective-permute-start | bytes 98312 | tf_op jit(solution)/shard_map/ppermute | solution.py:16
  51.5 6.6 %all-reduce.18 = (f32[1,32]{1,0:T(1,128)S(1)}, f32[1,32]{1,0:T(1,128)S(1)}) all-reduce(f32[1,32]{1,0:T(1,128)S(1)} %bitcast.534, f32[1,32]{1,0:T(1,128)S(1)} %bitcast.528), channel_id=1, replica_groups=mesh['dp'=32,'section'=4,'space'=4] {'space'}, use_global_device_ids=true, to_apply=%region_11.12 | all-reduce | flops 64 | bytes 512 | tf_op jit(solution)/shard_map/psum | solution.py:145
  62.9 2.8 collective-permute-done.3
  71.7 5.8 %all-reduce.17 = (f32[1,32]{1,0:T(1,128)S(1)}, f32[1,32]{1,0:T(1,128)S(1)}) all-reduce(f32[1,32]{1,0:T(1,128)S(1)} %bitcast.535, f32[1,32]{1,0:T(1,128)S(1)} %bitcast.529), channel_id=1, replica_groups=mesh['dp'=32,'section'=4,'space'=4] {'space'}, use_global_device_ids=true, to_apply=%region_17.18 | all-reduce | flops 64 | bytes 512 | tf_op jit(solution)/shard_map/psum | solution.py:145
  85.6 5.1 %collective-permute-start.8 = (bf16[1,1,64,256]{3,2,1,0:T(8,128)(2,1)S(1)}, bf16[1,1,64,256]{3,2,1,0:T(8,128)(2,1)S(1)}, u32[]{:S(2)}, u32[]{:S(2)}) collective-permute-start(bf16[1,1,64,256]{3,2,1,0:T(8,128)(2,1)S(1)} %fusion.5), channel_id=1, source_target_pairs={{0,4},{4,8},{8,12},{1,5},{5,9},{9,13},{2,6},{6,10},{10,14},{3,7},{... | collective-permute-start | bytes 98312 | tf_op jit(solution)/shard_map/ppermute | solution.py:16
  93.4 5.8 %all-reduce.16 = (f32[1,32]{1,0:T(1,128)S(1)}, f32[1,32]{1,0:T(1,128)S(1)}) all-reduce(f32[1,32]{1,0:T(1,128)S(1)} %bitcast.536, f32[1,32]{1,0:T(1,128)S(1)} %bitcast.530), channel_id=1, replica_groups=mesh['dp'=32,'section'=4,'space'=4] {'space'}, use_global_device_ids=true, to_apply=%region_23.24 | all-reduce | flops 64 | bytes 512 | tf_op jit(solution)/shard_map/psum | solution.py:145
  104.5 2.8 collective-permute-done.10
  108.6 5.8 %collective-permute-start.12 = (bf16[1,1,64,256]{3,2,1,0:T(8,128)(2,1)S(1)}, bf16[1,1,64,256]{3,2,1,0:T(8,128)(2,1)S(1)}, u32[]{:S(2)}, u32[]{:S(2)}) collective-permute-start(bf16[1,1,64,256]{3,2,1,0:T(8,128)(2,1)S(1)} %fusion.4), channel_id=1, source_target_pairs={{0,4},{4,8},{8,12},{1,5},{5,9},{9,13},{2,6},{6,10},{10,14},{3,7},{... | collective-permute-start | bytes 98312 | tf_op jit(solution)/shard_map/ppermute | solution.py:16
  117.0 5.8 %all-reduce.15 = (f32[1,32]{1,0:T(1,128)S(1)}, f32[1,32]{1,0:T(1,128)S(1)}) all-reduce(f32[1,32]{1,0:T(1,128)S(1)} %bitcast.537, f32[1,32]{1,0:T(1,128)S(1)} %bitcast.531), channel_id=1, replica_groups=mesh['dp'=32,'section'=4,'space'=4] {'space'}, use_global_device_ids=true, to_apply=%region_29.30 | all-reduce | flops 64 | bytes 512 | tf_op jit(solution)/shard_map/psum | solution.py:145
  126.3 5.8 %all-reduce.14 = (f32[1,32]{1,0:T(1,128)S(1)}, f32[32]{0:T(128)S(1)}) all-reduce(f32[1,32]{1,0:T(1,128)S(1)} %broadcast_multiply_fusion.3, f32[32]{0:T(128)S(1)} %get-tuple-element.70), channel_id=1, replica_groups=mesh['dp'=32,'section'=4,'space'=4] {'space'}, use_global_device_ids=true, to_apply=%region_35.36 | all-reduce | flops 64 | bytes 512 | tf_op jit(solution)/shard_map/psum | solution.py:210
  133.8 6.9 %collective-permute-done.18 = bf16[1,1,64,256]{3,2,1,0:T(8,128)(2,1)S(1)} collective-permute-done((bf16[1,1,64,256]{3,2,1,0:T(8,128)(2,1)S(1)}, bf16[1,1,64,256]{3,2,1,0:T(8,128)(2,1)S(1)}, u32[]{:S(2)}, u32[]{:S(2)}) %collective-permute-start.18) | collective-permute-done | bytes 32800 | tf_op jit(solution)/shard_map/ppermute | solution.py:16
  149.0 6.0 %all-reduce.13 = (f32[1,32]{1,0:T(1,128)S(1)}, f32[32]{0:T(128)S(1)}) all-reduce(f32[1,32]{1,0:T(1,128)S(1)} %broadcast_multiply_fusion.2, f32[32]{0:T(128)S(1)} %get-tuple-element.66), channel_id=1, replica_groups=mesh['dp'=32,'section'=4,'space'=4] {'space'}, use_global_device_ids=true, to_apply=%region_41.42 | all-reduce | flops 64 | bytes 512 | tf_op jit(solution)/shard_map/psum | solution.py:210
  156.7 6.8 %collective-permute-done.21 = bf16[1,1,64,256]{3,2,1,0:T(8,128)(2,1)S(1)} collective-permute-done((bf16[1,1,64,256]{3,2,1,0:T(8,128)(2,1)S(1)}, bf16[1,1,64,256]{3,2,1,0:T(8,128)(2,1)S(1)}, u32[]{:S(2)}, u32[]{:S(2)}) %collective-permute-start.21) | collective-permute-done | bytes 32800 | tf_op jit(solution)/shard_map/ppermute | solution.py:16
  172.2 6.9 %all-reduce.12 = (f32[1,32]{1,0:T(1,128)S(1)}, f32[32]{0:T(128)S(1)}) all-reduce(f32[1,32]{1,0:T(1,128)S(1)} %broadcast_multiply_fusion.1, f32[32]{0:T(128)S(1)} %get-tuple-element.62), channel_id=1, replica_groups=mesh['dp'=32,'section'=4,'space'=4] {'space'}, use_global_device_ids=true, to_apply=%region_47.48 | all-reduce | flops 64 | bytes 512 | tf_op jit(solution)/shard_map/psum | solution.py:210
  180.8 6.0 %collective-permute-done.24 = bf16[1,1,64,256]{3,2,1,0:T(8,128)(2,1)S(1)} collective-permute-done((bf16[1,1,64,256]{3,2,1,0:T(8,128)(2,1)S(1)}, bf16[1,1,64,256]{3,2,1,0:T(8,128)(2,1)S(1)}, u32[]{:S(2)}, u32[]{:S(2)}) %collective-permute-start.24) | collective-permute-done | bytes 32800 | tf_op jit(solution)/shard_map/ppermute | solution.py:16
  191.2 2.8 collective-permute-done.26
  195.0 5.8 %all-reduce.11 = (f32[1,32]{1,0:T(1,128)S(1)}, f32[32]{0:T(128)S(1)}) all-reduce(f32[1,32]{1,0:T(1,128)S(1)} %broadcast_multiply_fusion, f32[32]{0:T(128)S(1)} %get-tuple-element.58), channel_id=1, replica_groups=mesh['dp'=32,'section'=4,'space'=4] {'space'}, use_global_device_ids=true, to_apply=%region_53.54 | all-reduce | flops 64 | bytes 512 | tf_op jit(solution)/shard_map/psum | solution.py:210
  206.9 6.6 %collective-permute-done.28 = bf16[1,1,64,256]{3,2,1,0:T(8,128)(2,1)S(1)} collective-permute-done((bf16[1,1,64,256]{3,2,1,0:T(8,128)(2,1)S(1)}, bf16[1,1,64,256]{3,2,1,0:T(8,128)(2,1)S(1)}, u32[]{:S(2)}, u32[]{:S(2)}) %collective-permute-start.28) | collective-permute-done | bytes 32800 | tf_op jit(solution)/shard_map/ppermute | solution.py:16
  224.7 79.8 %all-reduce.26.cloned.1.call-done = (f32[1,3,3,256,256]{4,3,2,1,0:T(8,128)}, f32[1,256,512]{2,1,0:T(8,128)}) async-done(((f32[1,3,3,256,256]{4,3,2,1,0:T(8,128)}, f32[1,256,512]{2,1,0:T(8,128)}), (f32[1,3,3,256,256]{4,3,2,1,0:T(8,128)}, f32[1,256,512]{2,1,0:T(8,128)})) %all-reduce.26.cloned.1.call-update) | async-done | bytes 2883600 | tf_op jit(solution)/shard_map/psum | solution.py:223
  304.6 7.8 %psum.200 = f32[1,256]{1,0:T(1,128)S(1)} all-reduce(f32[1,256]{1,0:T(1,128)S(1)} %bitcast.511), channel_id=1, replica_groups=mesh['dp'=32,'section'=4,'space'=4] {'space'}, use_global_device_ids=true, to_apply=%region_61.62 | all-reduce | flops 256 | bytes 2048 | tf_op jit(solution)/shard_map/psum | solution.py:223
  312.3 75.2 %psum.201 = f32[1,256]{1,0:T(1,128)} all-reduce(f32[1,256]{1,0:T(1,128)S(1)} %psum.200), channel_id=1, replica_groups=mesh['dp'=32,'section'=4,'space'=4] {'dp'}, use_global_device_ids=true, to_apply=%region_62.63 | all-reduce | flops 256 | bytes 2048 | tf_op jit(solution)/shard_map/psum | solution.py:223
  387.6 91.5 %all-reduce.24.cloned.1.call-done = (f32[1,3,3,256,256]{4,3,2,1,0:T(8,128)}, f32[1,256,512]{2,1,0:T(8,128)}) async-done(((f32[1,3,3,256,256]{4,3,2,1,0:T(8,128)}, f32[1,256,512]{2,1,0:T(8,128)}), (f32[1,3,3,256,256]{4,3,2,1,0:T(8,128)}, f32[1,256,512]{2,1,0:T(8,128)})) %all-reduce.24.cloned.1.call-update) | async-done | bytes 2883600 | tf_op jit(solution)/shard_map/psum | solution.py:223
  479.1 3.3 copy.142
  (428 shorter events, 105.2 us)
Async XLA Ops:
  7.2 297.3 %all-reduce.26.cloned.1.call-start = ((), (), s32[]{:S(2)}) async-start(), calls=%async_computation.1 | async-start | bytes 5767168 | tf_op jit(solution)/shard_map/psum | solution.py:223
  8.0 36.7 %collective-permute-start.17 = (bf16[1,1,64,256]{3,2,1,0:T(8,128)(2,1)S(1)}, bf16[1,1,64,256]{3,2,1,0:T(8,128)(2,1)S(1)}, u32[]{:S(2)}, u32[]{:S(2)}) collective-permute-start(bf16[1,1,64,256]{3,2,1,0:T(8,128)(2,1)S(1)} %select_select_fusion.2), channel_id=1, source_target_pairs={{1,0},{2,1},{3,2},{5,4},{6,5},{7,6},{9,8},{10,9},{11,10},{13,12},{... | collective-permute-start | bytes 98312 | tf_op jit(solution)/shard_map/ppermute | solution.py:27
  9.9 34.8 %collective-permute-start.16 = (bf16[1,1,64,256]{3,2,1,0:T(8,128)(2,1)S(1)}, bf16[1,1,64,256]{3,2,1,0:T(8,128)(2,1)S(1)}, u32[]{:S(2)}, u32[]{:S(2)}) collective-permute-start(bf16[1,1,64,256]{3,2,1,0:T(8,128)(2,1)S(1)} %select_select_fusion.2), channel_id=1, source_target_pairs={{0,1},{1,2},{2,3},{4,5},{5,6},{6,7},{8,9},{9,10},{10,11},{12,13},{... | collective-permute-start | bytes 98312 | tf_op jit(solution)/shard_map/ppermute | solution.py:26
  26.9 9.0 %collective-permute-start.1 = (bf16[1,1,64,256]{3,2,1,0:T(8,128)(2,1)S(1)}, bf16[1,1,64,256]{3,2,1,0:T(8,128)(2,1)S(1)}, u32[]{:S(2)}, u32[]{:S(2)}) collective-permute-start(bf16[1,1,64,256]{3,2,1,0:T(8,128)(2,1)S(1)} %multiply_convert_fusion.4), channel_id=1, source_target_pairs={{1,0},{2,1},{3,2},{5,4},{6,5},{7,6},{9,8},{10,9},{11,10},{13,12},{... | collective-permute-start | bytes 98312 | tf_op jit(solution)/shard_map/ppermute | solution.py:27
  28.8 7.1 %collective-permute-start = (bf16[1,1,64,256]{3,2,1,0:T(8,128)(2,1)S(1)}, bf16[1,1,64,256]{3,2,1,0:T(8,128)(2,1)S(1)}, u32[]{:S(2)}, u32[]{:S(2)}) collective-permute-start(bf16[1,1,64,256]{3,2,1,0:T(8,128)(2,1)S(1)} %multiply_convert_fusion.4), channel_id=1, source_target_pairs={{0,1},{1,2},{2,3},{4,5},{5,6},{6,7},{8,9},{9,10},{10,11},{12,13},{... | collective-permute-start | bytes 98312 | tf_op jit(solution)/shard_map/ppermute | solution.py:26
  36.9 53.9 %collective-permute-start.9 = (bf16[1,1,64,256]{3,2,1,0:T(8,128)(2,1)S(1)}, bf16[1,1,64,256]{3,2,1,0:T(8,128)(2,1)S(1)}, u32[]{:S(2)}, u32[]{:S(2)}) collective-permute-start(bf16[1,1,64,256]{3,2,1,0:T(8,128)(2,1)S(1)} %fusion.8), channel_id=1, source_target_pairs={{0,12},{1,13},{2,14},{3,15},{16,28},{17,29},{18,30},{19,31},{32,44... | collective-permute-start | bytes 98312 | tf_op jit(solution)/shard_map/ppermute | solution.py:16
  43.4 7.0 %collective-permute-start.2 = (bf16[1,1,64,256]{3,2,1,0:T(8,128)(2,1)S(1)}, bf16[1,1,64,256]{3,2,1,0:T(8,128)(2,1)S(1)}, u32[]{:S(2)}, u32[]{:S(2)}) collective-permute-start(bf16[1,1,64,256]{3,2,1,0:T(8,128)(2,1)S(1)} %fusion.8), channel_id=1, source_target_pairs={{0,4},{4,8},{8,12},{1,5},{5,9},{9,13},{2,6},{6,10},{10,14},{3,7},{... | collective-permute-start | bytes 98312 | tf_op jit(solution)/shard_map/ppermute | solution.py:16
  66.2 48.7 %collective-permute-start.13 = (bf16[1,1,64,256]{3,2,1,0:T(8,128)(2,1)S(1)}, bf16[1,1,64,256]{3,2,1,0:T(8,128)(2,1)S(1)}, u32[]{:S(2)}, u32[]{:S(2)}) collective-permute-start(bf16[1,1,64,256]{3,2,1,0:T(8,128)(2,1)S(1)} %fusion.6), channel_id=1, source_target_pairs={{0,12},{1,13},{2,14},{3,15},{16,28},{17,29},{18,30},{19,31},{32,44... | collective-permute-start | bytes 98312 | tf_op jit(solution)/shard_map/ppermute | solution.py:16
  85.6 6.7 %collective-permute-start.8 = (bf16[1,1,64,256]{3,2,1,0:T(8,128)(2,1)S(1)}, bf16[1,1,64,256]{3,2,1,0:T(8,128)(2,1)S(1)}, u32[]{:S(2)}, u32[]{:S(2)}) collective-permute-start(bf16[1,1,64,256]{3,2,1,0:T(8,128)(2,1)S(1)} %fusion.5), channel_id=1, source_target_pairs={{0,4},{4,8},{8,12},{1,5},{5,9},{9,13},{2,6},{6,10},{10,14},{3,7},{... | collective-permute-start | bytes 98312 | tf_op jit(solution)/shard_map/ppermute | solution.py:16
  108.6 7.3 %collective-permute-start.12 = (bf16[1,1,64,256]{3,2,1,0:T(8,128)(2,1)S(1)}, bf16[1,1,64,256]{3,2,1,0:T(8,128)(2,1)S(1)}, u32[]{:S(2)}, u32[]{:S(2)}) collective-permute-start(bf16[1,1,64,256]{3,2,1,0:T(8,128)(2,1)S(1)} %fusion.4), channel_id=1, source_target_pairs={{0,4},{4,8},{8,12},{1,5},{5,9},{9,13},{2,6},{6,10},{10,14},{3,7},{... | collective-permute-start | bytes 98312 | tf_op jit(solution)/shard_map/ppermute | solution.py:16
  132.5 8.3 %collective-permute-start.18 = (bf16[1,1,64,256]{3,2,1,0:T(8,128)(2,1)S(1)}, bf16[1,1,64,256]{3,2,1,0:T(8,128)(2,1)S(1)}, u32[]{:S(2)}, u32[]{:S(2)}) collective-permute-start(bf16[1,1,64,256]{3,2,1,0:T(8,128)(2,1)S(1)} %fusion.123), channel_id=1, source_target_pairs={{4,0},{8,4},{12,8},{5,1},{9,5},{13,9},{6,2},{10,6},{14,10},{7,3},{... | collective-permute-start | bytes 98312 | tf_op jit(solution)/shard_map/ppermute | solution.py:16
  140.8 6.0 %collective-permute-start.20 = (bf16[1,1,64,256]{3,2,1,0:T(8,128)(2,1)S(1)}, bf16[1,1,64,256]{3,2,1,0:T(8,128)(2,1)S(1)}, u32[]{:S(2)}, u32[]{:S(2)}) collective-permute-start(bf16[1,1,64,256]{3,2,1,0:T(8,128)(2,1)S(1)} %select_select_fusion.1), channel_id=1, source_target_pairs={{1,0},{2,1},{3,2},{5,4},{6,5},{7,6},{9,8},{10,9},{11,10},{13,12},{... | collective-permute-start | bytes 98312 | tf_op jit(solution)/shard_map/ppermute | solution.py:27
  145.1 35.7 %collective-permute-start.25 = (bf16[1,1,64,256]{3,2,1,0:T(8,128)(2,1)S(1)}, bf16[1,1,64,256]{3,2,1,0:T(8,128)(2,1)S(1)}, u32[]{:S(2)}, u32[]{:S(2)}) collective-permute-start(bf16[1,1,64,256]{3,2,1,0:T(8,128)(2,1)S(1)} %fusion.123), channel_id=1, source_target_pairs={{12,0},{13,1},{14,2},{15,3},{28,16},{29,17},{30,18},{31,19},{44,32... | collective-permute-start | bytes 98312 | tf_op jit(solution)/shard_map/ppermute | solution.py:16
  155.4 8.1 %collective-permute-start.21 = (bf16[1,1,64,256]{3,2,1,0:T(8,128)(2,1)S(1)}, bf16[1,1,64,256]{3,2,1,0:T(8,128)(2,1)S(1)}, u32[]{:S(2)}, u32[]{:S(2)}) collective-permute-start(bf16[1,1,64,256]{3,2,1,0:T(8,128)(2,1)S(1)} %fusion.75), channel_id=1, source_target_pairs={{4,0},{8,4},{12,8},{5,1},{9,5},{13,9},{6,2},{10,6},{14,10},{7,3},{... | collective-permute-start | bytes 98312 | tf_op jit(solution)/shard_map/ppermute | solution.py:16
  163.5 7.6 %collective-permute-start.23 = (bf16[1,1,64,256]{3,2,1,0:T(8,128)(2,1)S(1)}, bf16[1,1,64,256]{3,2,1,0:T(8,128)(2,1)S(1)}, u32[]{:S(2)}, u32[]{:S(2)}) collective-permute-start(bf16[1,1,64,256]{3,2,1,0:T(8,128)(2,1)S(1)} %select_select_fusion), channel_id=1, source_target_pairs={{1,0},{2,1},{3,2},{5,4},{6,5},{7,6},{9,8},{10,9},{11,10},{13,12},{... | collective-permute-start | bytes 98312 | tf_op jit(solution)/shard_map/ppermute | solution.py:27
  165.5 5.7 %collective-permute-start.22 = (bf16[1,1,64,256]{3,2,1,0:T(8,128)(2,1)S(1)}, bf16[1,1,64,256]{3,2,1,0:T(8,128)(2,1)S(1)}, u32[]{:S(2)}, u32[]{:S(2)}) collective-permute-start(bf16[1,1,64,256]{3,2,1,0:T(8,128)(2,1)S(1)} %select_select_fusion), channel_id=1, source_target_pairs={{0,1},{1,2},{2,3},{4,5},{5,6},{6,7},{8,9},{9,10},{10,11},{12,13},{... | collective-permute-start | bytes 98312 | tf_op jit(solution)/shard_map/ppermute | solution.py:26
  169.8 37.1 %collective-permute-start.29 = (bf16[1,1,64,256]{3,2,1,0:T(8,128)(2,1)S(1)}, bf16[1,1,64,256]{3,2,1,0:T(8,128)(2,1)S(1)}, u32[]{:S(2)}, u32[]{:S(2)}) collective-permute-start(bf16[1,1,64,256]{3,2,1,0:T(8,128)(2,1)S(1)} %fusion.75), channel_id=1, source_target_pairs={{12,0},{13,1},{14,2},{15,3},{28,16},{29,17},{30,18},{31,19},{44,32... | collective-permute-start | bytes 98312 | tf_op jit(solution)/shard_map/ppermute | solution.py:16
  179.5 7.3 %collective-permute-start.24 = (bf16[1,1,64,256]{3,2,1,0:T(8,128)(2,1)S(1)}, bf16[1,1,64,256]{3,2,1,0:T(8,128)(2,1)S(1)}, u32[]{:S(2)}, u32[]{:S(2)}) collective-permute-start(bf16[1,1,64,256]{3,2,1,0:T(8,128)(2,1)S(1)} %fusion.79), channel_id=1, source_target_pairs={{4,0},{8,4},{12,8},{5,1},{9,5},{13,9},{6,2},{10,6},{14,10},{7,3},{... | collective-permute-start | bytes 98312 | tf_op jit(solution)/shard_map/ppermute | solution.py:16
  201.2 16.8 %collective-permute-start.15 = (bf16[1,1,64,256]{3,2,1,0:T(8,128)(2,1)S(1)}, bf16[1,1,64,256]{3,2,1,0:T(8,128)(2,1)S(1)}, u32[]{:S(2)}, u32[]{:S(2)}) collective-permute-start(bf16[1,1,64,256]{3,2,1,0:T(8,128)(2,1)S(1)} %get-tuple-element.120), channel_id=1, source_target_pairs={{1,0},{2,1},{3,2},{5,4},{6,5},{7,6},{9,8},{10,9},{11,10},{13,12},{... | collective-permute-start | bytes 98312 | tf_op jit(solution)/shard_map/ppermute | solution.py:27
  203.1 14.9 %collective-permute-start.14 = (bf16[1,1,64,256]{3,2,1,0:T(8,128)(2,1)S(1)}, bf16[1,1,64,256]{3,2,1,0:T(8,128)(2,1)S(1)}, u32[]{:S(2)}, u32[]{:S(2)}) collective-permute-start(bf16[1,1,64,256]{3,2,1,0:T(8,128)(2,1)S(1)} %get-tuple-element.120), channel_id=1, source_target_pairs={{0,1},{1,2},{2,3},{4,5},{5,6},{6,7},{8,9},{9,10},{10,11},{12,13},{... | collective-permute-start | bytes 98312 | tf_op jit(solution)/shard_map/ppermute | solution.py:26
  205.6 7.9 %collective-permute-start.28 = (bf16[1,1,64,256]{3,2,1,0:T(8,128)(2,1)S(1)}, bf16[1,1,64,256]{3,2,1,0:T(8,128)(2,1)S(1)}, u32[]{:S(2)}, u32[]{:S(2)}) collective-permute-start(bf16[1,1,64,256]{3,2,1,0:T(8,128)(2,1)S(1)} %get-tuple-element.119), channel_id=1, source_target_pairs={{4,0},{8,4},{12,8},{5,1},{9,5},{13,9},{6,2},{10,6},{14,10},{7,3},{... | collective-permute-start | bytes 98312 | tf_op jit(solution)/shard_map/ppermute | solution.py:16
  213.5 9.4 %collective-permute-start.31 = (bf16[1,1,64,256]{3,2,1,0:T(8,128)(2,1)S(1)}, bf16[1,1,64,256]{3,2,1,0:T(8,128)(2,1)S(1)}, u32[]{:S(2)}, u32[]{:S(2)}) collective-permute-start(bf16[1,1,64,256]{3,2,1,0:T(8,128)(2,1)S(1)} %fusion.122), channel_id=1, source_target_pairs={{1,0},{2,1},{3,2},{5,4},{6,5},{7,6},{9,8},{10,9},{11,10},{13,12},{... | collective-permute-start | bytes 98312 | tf_op jit(solution)/shard_map/ppermute | solution.py:27
  215.8 7.1 %collective-permute-start.30 = (bf16[1,1,64,256]{3,2,1,0:T(8,128)(2,1)S(1)}, bf16[1,1,64,256]{3,2,1,0:T(8,128)(2,1)S(1)}, u32[]{:S(2)}, u32[]{:S(2)}) collective-permute-start(bf16[1,1,64,256]{3,2,1,0:T(8,128)(2,1)S(1)} %fusion.122), channel_id=1, source_target_pairs={{0,1},{1,2},{2,3},{4,5},{5,6},{6,7},{8,9},{9,10},{10,11},{12,13},{... | collective-permute-start | bytes 98312 | tf_op jit(solution)/shard_map/ppermute | solution.py:26
  224.6 254.4 %all-reduce.24.cloned.1.call-start = ((), (), s32[]{:S(2)}) async-start(), calls=%async_computation | async-start | bytes 5767168 | tf_op jit(solution)/shard_map/psum | solution.py:223
  (38 other events, 319.6 us)
Sparse Core Ops, SparseCore 0:
  224.8 79.7 all-reduce.25
  308.2 170.8 all-reduce.23
